TPU v7x, 256 devices: a whole 4x4x8 slice. The times are simulated.
256 devices in a mesh: day: 8 (over x, core), row: 32 (over y, z).
Axes of the slice: x: 4, y: 4, z: 8, core: 2. Of those that a mesh axis runs over, the one named last changes fastest.
Arguments:
- features: bfloat16 [8, 768, 16, 128, 128], P('day', 'row'), may hold values from -6 to 6
- blocks: int32 [8, 768, 16], P('day', 'row'), may hold values from 0 to 255, as said below
- labels: int32 [8, 768, 128], P('day', 'row'), may hold values from 0 to 15
- coef: float32 [8, 16, 32768], P('day', None, 'row'), may hold values from -0.125 to 0.125
- direction: float32 [8, 16, 32768], P('day', None, 'row'), may hold values from -0.125 to 0.125
- prior: float32 [32768], P('row'), may hold values from 100 to 3000
Outputs:
- gradient: float32 [8, 16, 32768], P('day', None, 'row')
- hess_dir: float32 [8, 16, 32768], P('day', None, 'row')
Inputs may be any that keep to these rules, and one draw needn't show every extreme that they name: `blocks`: within one row tile the 16 block numbers are distinct.
All inputs are finite; a program needn't handle non-finite values.
Results may differ from a plain program's by a relative error of at most 0.0003.
Values may be sent and summed in bfloat16 or wider, within the bound.
No kernel may reach another device: no remote copies, remote signals or barrier semaphores. Data moves between devices by JAX's collectives and lax.ppermute only.
A program may use at most 64 MiB of HBM per device.

v0:
```python
import jax
import jax.numpy as jnp
from jax import lax
from jax.sharding import Mesh
from jax.sharding import PartitionSpec as P

ROW = ("row_0", "row_1")


def extended(cells, sides, width):
    for axis, dim in sides:
        count = lax.axis_size(axis)
        ends = count - 1
        head = lax.slice_in_dim(cells, 0, width, axis=dim)
        tail = lax.slice_in_dim(cells, cells.shape[dim] - width, cells.shape[dim], axis=dim)
        cells = jnp.concatenate(
            [
                lax.ppermute(tail, axis, [(i, (i + 1) % count) for i in range(ends)]),
                cells,
                lax.ppermute(head, axis, [((i + 1) % count, i) for i in range(ends)]),
            ],
            axis=dim,
        )
    return cells


def on_device(features, blocks, labels, coef, direction, prior):
    arms = coef.shape[1]
    width = features.shape[-1]
    coef_pair = jnp.concatenate([coef[0], direction[0]], axis=0).astype(jnp.bfloat16)
    coef_table = lax.all_gather(coef_pair, ROW, axis=1, tiled=True)
    nfeat = coef_table.shape[1]
    nblk = nfeat // width
    both = jnp.concatenate([coef, direction], axis=1)
    neighbours = extended(both, (("day", 0),), 1)
    blks = blocks[0]
    selected = coef_table.reshape(2 * arms, nblk, width)[:, blks]
    feats = features[0]
    logits_dir = jnp.einsum("tari,ktai->tkr", feats, selected, preferred_element_type=jnp.float32)
    logits = logits_dir[:, :arms]
    lin_dir = logits_dir[:, arms:]
    expo = jnp.exp(logits)
    probs = expo / jnp.sum(expo, axis=1, keepdims=True)
    onehot = (labels[0][:, None, :] == jnp.arange(arms, dtype=jnp.int32)[None, :, None]).astype(
        jnp.float32
    )
    resid = probs - onehot
    hrow = probs * lin_dir - probs * jnp.sum(probs * lin_dir, axis=1, keepdims=True)
    both_low = jnp.concatenate([resid, hrow], axis=1).astype(jnp.bfloat16)
    contrib = jnp.einsum("tari,tkr->taki", feats, both_low, preferred_element_type=jnp.float32)
    contrib = contrib.reshape(-1, 2 * arms, width)
    top = lax.reduce_precision(contrib, exponent_bits=8, mantissa_bits=7)
    hi = top.astype(jnp.bfloat16)
    lo = (contrib - top).astype(jnp.bfloat16)
    place = (blks.reshape(-1)[:, None] == jnp.arange(nblk, dtype=jnp.int32)[None, :]).astype(
        jnp.bfloat16
    )
    parts = jnp.einsum(
        "pb,pjki->jkbi", place, jnp.stack([hi, lo], axis=1), preferred_element_type=jnp.float32
    )
    partial_terms = parts[0] + parts[1]
    partial_terms = partial_terms.reshape(2 * arms, nfeat)
    owned = lax.psum_scatter(partial_terms, ROW, scatter_dimension=1, tiled=True)
    day_index = lax.axis_index("day")
    ndays = lax.axis_size("day")
    links = (day_index > 0).astype(jnp.float32) + (day_index < ndays - 1).astype(jnp.float32)
    coupling = links * neighbours[1] - neighbours[0] - neighbours[2]
    result = owned + prior[None, :] * coupling
    return (result[None, :arms], result[None, arms:])


def solution(mesh):
    finer = Mesh(mesh.devices.reshape(mesh.shape["day"], 4, 8), ("day", "row_0", "row_1"))
    return jax.shard_map(
        on_device,
        mesh=finer,
        in_specs=(
            P("day", ROW, None, None, None),
            P("day", ROW, None),
            P("day", ROW, None),
            P("day", None, ROW),
            P("day", None, ROW),
            P(ROW),
        ),
        out_specs=(P("day", None, ROW), P("day", None, ROW)),
        check_vma=False,
    )
```

profile of v0, /device:TPU:4, one launch (start us, length us, event | category | flops | bytes accessed | tf_op | source)
XLA Modules:
  0.0 374.2 jit_solution(4076354408150905320)
XLA Ops:
  7.2 0.0 all-gather.2.cloned.1.call-start
  7.2 0.9 constant_dynamic-update-slice_fusion.1
  8.1 0.9 constant_dynamic-update-slice_fusion
  9.1 0.6 pad_maximum_fusion
  9.7 0.0 all-gather.2.cloned.1.call-update
  9.7 0.0 reduce-scatter.2.cloned.1.call-start
  9.8 0.8 copy.20
  10.5 0.7 compare_select_fusion
  11.2 0.1 copy.16
  11.3 0.1 reshape.84
  11.4 0.1 eq.34
  11.5 80.7 %all-gather.2.cloned.1.call-done = bf16[32,32768]{1,0:T(8,128)(2,1)} async-done(((bf16[32,1024]{1,0:T(8,128)(2,1)}), bf16[32,32768]{1,0:T(8,128)(2,1)}) %all-gather.2.cloned.1.call-update) | async-done | bytes 2097168 | tf_op jit(solution)/shard_map/all_gather | solution.py:31
  92.2 2.0 copy_bitcast_fusion.1
  94.2 3.2 gather_fusion
  97.3 9.7 %fusion.14 = f32[24,32,128]{2,1,0:T(8,128)S(1)} fusion(bf16[32,24,16,128]{3,0,2,1:T(8,128)(2,1)} %bitcast.59, bf16[1,24,16,128,128]{4,3,2,1,0:T(8,128)(2,1)} %param.6), kind=kOutput, calls=%fused_computation.18 | convolution fusion | flops 402653184 | bytes 16121856 | tf_op jit(solution)/shard_map/tari,ktai->tkr/dot_general | solution.py:39
  107.0 0.8 subtract_convert_fusion
  107.8 0.1 fusion.20
  107.9 9.0 %fusion.2 = f32[24,32,16,128]{3,1,2,0:T(8,128)} fusion(bf16[1,24,16,128,128]{4,3,2,1,0:T(8,128)(2,1)} %param.6, bf16[24,16,128]{2,1,0:T(8,128)(2,1)S(1)} %fusion.20, bf16[24,16,128]{2,1,0:T(8,128)(2,1)S(1)} %get-tuple-element.10), kind=kOutput, calls=%fused_computation.3 | convolution fusion | flops 403046400 | bytes 19070976 | tf_op jit(solution)/shard_map/tari,tkr->taki/dot_general | solution.py:50
  116.9 6.6 %copy.18 = f32[384,1,32,128]{0,3,2,1:T(8,128)} copy(f32[384,1,32,128]{3,2,0,1:T(8,128)} %bitcast.56) | data formatting | bytes 12582912 | tf_op jit(solution)/shard_map/reshape | solution.py:51
  123.4 4.3 %reduce-precision_convert_fusion = (bf16[384,1,32,128]{0,3,2,1:T(8,128)(2,1)S(1)}, bf16[384,1,32,128]{0,3,2,1:T(8,128)(2,1)S(1)}) fusion(f32[384,1,32,128]{0,3,2,1:T(8,128)} %copy.18), kind=kLoop, calls=%fused_computation.8 | loop fusion | flops 6291456 | bytes 12582912 | tf_op jit(solution)/shard_map/convert_element_type | solution.py:53
  127.7 2.5 fusion.11
  130.2 2.8 slice_add_fusion
  132.9 5.6 %copy.21 = f32[1,32,256,128]{3,2,1,0:T(8,128)} copy(f32[1,32,256,128]{2,3,1,0:T(8,128)} %slice_add_fusion) | data formatting | bytes 8388608 | tf_op jit(solution)/shard_map/add | solution.py:61
  138.5 6.6 %copy.29 = f32[4,8,256,128]{3,1,2,0:T(8,128)} copy(f32[4,8,256,128]{3,2,1,0:T(8,128)} %bitcast.58) | data formatting | bytes 8388608
  145.1 0.0 reduce-scatter.2.cloned.1.call-update
  145.1 1.9 collective-permute-start
  147.0 3.6 collective-permute-start.1
  150.7 0.7 collective-permute-done
  151.4 1.8 collective-permute-done.1
  153.2 212.6 %reduce-scatter.2.cloned.1.call-done = f32[32,1024]{1,0:T(8,128)} async-done(((f32[32,32768]{1,0:T(8,128)}), f32[32,1024]{1,0:T(8,128)}) %reduce-scatter.2.cloned.1.call-update) | async-done | bytes 131088 | tf_op jit(solution)/shard_map/reduce_scatter | solution.py:63
  365.8 0.9 fusion.28
  366.7 0.7 slice_bitcast_fusion
  (5 shorter events, 0.0 us)
Async XLA Ops:
  7.2 85.1 %all-gather.2.cloned.1.call-start = ((), (), s32[]{:S(2)}) async-start(), calls=%async_computation.1 | async-start | bytes 2162688 | tf_op jit(solution)/shard_map/all_gather | solution.py:31
  9.7 356.0 %reduce-scatter.2.cloned.1.call-start = ((), (), s32[]{:S(2)}) async-start(), calls=%async_computation.2 | async-start | bytes 4325376 | tf_op jit(solution)/shard_map/reduce_scatter | solution.py:63
  97.3 9.7 %copy-start.1 = (s32[1,24,128]{2,1,0:T(8,128)S(1)}, s32[1,24,128]{2,1,0:T(8,128)}, u32[]{:S(2)}) copy-start(s32[1,24,128]{2,1,0:T(8,128)} %param.8) | copy-start | bytes 36868
  145.1 220.7 %copy-start = (f32[1024]{0:T(1024)S(1)}, f32[1024]{0:T(1024)}, u32[]{:S(2)}) copy-start(f32[1024]{0:T(1024)} %param.11) | copy-start | bytes 12292
  145.1 6.3 %collective-permute-start = (f32[1,32,1024]{2,1,0:T(8,128)S(1)}, f32[1,32,1024]{2,1,0:T(8,128)S(1)}, u32[]{:S(2)}, u32[]{:S(2)}) collective-permute-start(f32[1,32,1024]{2,1,0:T(8,128)S(1)} %get-tuple-element.6), channel_id=1, source_target_pairs={{0,32},{32,64},{64,96},{96,128},{128,160},{160,192},{192,224},{1,3... | collective-permute-start | bytes 393224 | tf_op jit(solution)/shard_map/ppermute | solution.py:18
  147.0 6.1 %collective-permute-start.1 = (f32[1,32,1024]{2,1,0:T(8,128)S(1)}, f32[1,32,1024]{2,1,0:T(8,128)S(1)}, u32[]{:S(2)}, u32[]{:S(2)}) collective-permute-start(f32[1,32,1024]{2,1,0:T(8,128)S(1)} %get-tuple-element.6), channel_id=1, source_target_pairs={{32,0},{64,32},{96,64},{128,96},{160,128},{192,160},{224,192},{33,... | collective-permute-start | bytes 393224 | tf_op jit(solution)/shard_map/ppermute | solution.py:20
Sparse Core Ops, SparseCore 0:
  11.1 81.0 all-gather.1
  145.2 220.4 reduce-scatter.1
where the time goes:
time: 375 us; the launch traced here: 374 us
  waiting for transfers between devices  296 us (79%)
  local copies, waits for them, and re-layouts  25.5 us (7%)
  matrix products  21.1 us (6%)
  between operations  14.1 us (4%)
  other arithmetic  12 us (3%)
  starting transfers between devices  5.64 us (2%)
    reduce_scatter x1, waiting for transfers between devices, on_device(): lax.psum_scatter(partial_terms, ROW, scatter_dimension=1, tiled=True)  213 us
    all_gather x1, waiting for transfers between devices, on_device(): coef_table = lax.all_gather(coef_pair, ROW, axis=1, tiled=True)  80.7 us
    dot_general x1, matrix products, on_device(): jnp.einsum('tari,ktai->tkr', feats, selected, preferred_element_type=jnp....  9.67 us
    dot_general x1, matrix products, on_device(): jnp.einsum('tari,tkr->taki', feats, both_low, preferred_element_type=jnp....  9.02 us
  transfers between devices with their start and end apart: 4, of which 4 were waited for; matrix products, arithmetic and copies ran while one was open for 0% of the time, Pallas kernels for 0%

commit v1 on v0

--- a/solution.py
+++ b/solution.py
@@ -28,7 +28,9 @@
     arms = coef.shape[1]
     width = features.shape[-1]
     coef_pair = jnp.concatenate([coef[0], direction[0]], axis=0).astype(jnp.bfloat16)
-    coef_table = lax.all_gather(coef_pair, ROW, axis=1, tiled=True)
+    coef_table = jnp.concatenate(
+        lax.all_to_all(jnp.stack([coef_pair] * lax.axis_size(ROW)), ROW, 0, 0), axis=1
+    )
     nfeat = coef_table.shape[1]
     nblk = nfeat // width
     both = jnp.concatenate([coef, direction], axis=1)

time: 375 us -> 363 us (0.968)
  waiting for transfers between devices: 296 us -> 265 us
  starting transfers between devices: 5.64 us -> 17.1 us
  local copies, waits for them, and re-layouts: 25.5 us -> 34.1 us
    all_gather x1 -> x0, waiting for transfers between devices: 80.7 us -> none  [on_device(): coef_table = lax.all_gather(coef_pair, ROW, axis=1, tiled=True)]
    all_to_all x0 -> x1, waiting for transfers between devices: none -> 49.7 us  [on_device(): lax.all_to_all(jnp.stack([coef_pair] * lax.axis_size(ROW)), ROW, 0, 0)]
    all_to_all x0 -> x1, starting transfers between devices: none -> 11.5 us  [on_device(): lax.all_to_all(jnp.stack([coef_pair] * lax.axis_size(ROW)), ROW, 0, 0)]
    another operation x0 -> x3, local copies, waits for them, and re-layouts: none -> 8.72 us  [the longest x2 7.11 us: on_device(): selected = coef_table.reshape(2 * arms, nblk, width)[:, blks]]
where the time goes in v1:
time: 363 us
  waiting for transfers between devices  265 us (73%)
  local copies, waits for them, and re-layouts  34.1 us (9%)
  matrix products  21.1 us (6%)
  starting transfers between devices  17.1 us (5%)
  between operations  14.1 us (4%)
  other arithmetic  10.7 us (3%)
    reduce_scatter x1, waiting for transfers between devices, on_device(): lax.psum_scatter(partial_terms, ROW, scatter_dimension=1, tiled=True)  213 us
    all_to_all x1, waiting for transfers between devices, on_device(): lax.all_to_all(jnp.stack([coef_pair] * lax.axis_size(ROW)), ROW, 0, 0)  49.7 us
    all_to_all x1, starting transfers between devices, on_device(): lax.all_to_all(jnp.stack([coef_pair] * lax.axis_size(ROW)), ROW, 0, 0)  11.5 us
    dot_general x1, matrix products, on_device(): jnp.einsum('tari,ktai->tkr', feats, selected, preferred_element_type=jnp....  9.68 us
    dot_general x1, matrix products, on_device(): jnp.einsum('tari,tkr->taki', feats, both_low, preferred_element_type=jnp....  9.02 us
  transfers between devices with their start and end apart: 4, of which 4 were waited for; matrix products, arithmetic and copies ran while one was open for 0% of the time, Pallas kernels for 0%

profile of v1, /device:TPU:4, one launch (start us, length us, event | category | flops | bytes accessed | tf_op | source)
XLA Modules:
  0.0 362.6 jit_solution(11525260892043002913)
XLA Ops:
  7.2 0.9 constant_dynamic-update-slice_fusion.1
  8.1 0.9 constant_dynamic-update-slice_fusion
  9.0 1.6 stack.4
  10.7 11.5 %all-to-all-start = ((bf16[32,32,1024]{2,1,0:T(8,128)(2,1)}), bf16[32,32,1024]{2,1,0:T(8,128)(2,1)S(1)}, u32[]{:S(2)}, u32[]{:S(2)}) async-start(bf16[32,32,1024]{2,1,0:T(8,128)(2,1)} %stack.4), calls=%async_computation | async-start | bytes 4194304 | tf_op jit(solution)/shard_map/all_to_all | solution.py:32
  22.2 0.0 reduce-scatter.2.cloned.1.call-start
  22.2 0.1 copy.21
  22.3 0.1 copy.17
  22.4 0.1 reshape.95
  22.4 0.1 eq.34
  22.5 49.7 %all-to-all-done = bf16[32,32,1024]{2,1,0:T(8,128)(2,1)S(1)} async-done(((bf16[32,32,1024]{2,1,0:T(8,128)(2,1)}), bf16[32,32,1024]{2,1,0:T(8,128)(2,1)S(1)}, u32[]{:S(2)}, u32[]{:S(2)}) %all-to-all-start) | async-done | bytes 2097184 | tf_op jit(solution)/shard_map/all_to_all | solution.py:32
  72.2 2.5 copy.16
  74.7 4.2 %reshape_reshape.3 = bf16[32,256,128]{2,1,0:T(8,128)(2,1)} reshape(bf16[32,32,1024]{2,1,0:T(8,128)(2,1)} %copy.16) | data formatting | bytes 4194304 | tf_op jit(solution)/shard_map/reshape;reshape | solution.py:39
  78.9 2.9 copy.18
  81.8 3.2 gather_fusion
  85.0 9.7 %fusion.14 = f32[24,32,128]{2,1,0:T(8,128)S(1)} fusion(bf16[32,24,16,128]{3,0,2,1:T(8,128)(2,1)} %bitcast.55, bf16[1,24,16,128,128]{4,3,2,1,0:T(8,128)(2,1)} %param.6), kind=kOutput, calls=%fused_computation.17 | convolution fusion | flops 402653184 | bytes 16121856 | tf_op jit(solution)/shard_map/tari,ktai->tkr/dot_general | solution.py:41
  94.7 0.8 subtract_convert_fusion
  95.4 0.1 fusion.20
  95.5 9.0 %fusion.2 = f32[24,32,16,128]{3,1,2,0:T(8,128)} fusion(bf16[1,24,16,128,128]{4,3,2,1,0:T(8,128)(2,1)} %param.6, bf16[24,16,128]{2,1,0:T(8,128)(2,1)S(1)} %fusion.20, bf16[24,16,128]{2,1,0:T(8,128)(2,1)S(1)} %get-tuple-element.10), kind=kOutput, calls=%fused_computation.3 | convolution fusion | flops 403046400 | bytes 19070976 | tf_op jit(solution)/shard_map/tari,tkr->taki/dot_general | solution.py:52
  104.5 6.6 %copy.19 = f32[384,1,32,128]{0,3,2,1:T(8,128)} copy(f32[384,1,32,128]{3,2,0,1:T(8,128)} %bitcast.52) | data formatting | bytes 12582912 | tf_op jit(solution)/shard_map/reshape | solution.py:53
  111.1 4.3 %reduce-precision_convert_fusion = (bf16[384,1,32,128]{0,3,2,1:T(8,128)(2,1)S(1)}, bf16[384,1,32,128]{0,3,2,1:T(8,128)(2,1)S(1)}) fusion(f32[384,1,32,128]{0,3,2,1:T(8,128)} %copy.19), kind=kLoop, calls=%fused_computation.8 | loop fusion | flops 6291456 | bytes 12582912 | tf_op jit(solution)/shard_map/convert_element_type | solution.py:55
  115.4 2.5 fusion.11
  117.8 2.8 slice_add_fusion
  120.6 5.6 %copy.22 = f32[1,32,256,128]{3,2,1,0:T(8,128)} copy(f32[1,32,256,128]{2,3,1,0:T(8,128)} %slice_add_fusion) | data formatting | bytes 8388608 | tf_op jit(solution)/shard_map/add | solution.py:63
  126.1 6.6 %copy.28 = f32[4,8,256,128]{3,1,2,0:T(8,128)} copy(f32[4,8,256,128]{3,2,1,0:T(8,128)} %bitcast.54) | data formatting | bytes 8388608
  132.7 0.0 reduce-scatter.2.cloned.1.call-update
  132.8 1.9 collective-permute-start
  134.7 3.6 %collective-permute-start.1 = (f32[1,32,1024]{2,1,0:T(8,128)S(1)}, f32[1,32,1024]{2,1,0:T(8,128)S(1)}, u32[]{:S(2)}, u32[]{:S(2)}) collective-permute-start(f32[1,32,1024]{2,1,0:T(8,128)S(1)} %get-tuple-element.6), channel_id=1, source_target_pairs={{32,0},{64,32},{96,64},{128,96},{160,128},{192,160},{224,192},{33,... | collective-permute-start | bytes 393224 | tf_op jit(solution)/shard_map/ppermute | solution.py:20
  138.3 0.7 collective-permute-done
  139.0 1.8 collective-permute-done.1
  140.8 213.3 %reduce-scatter.2.cloned.1.call-done = f32[32,1024]{1,0:T(8,128)} async-done(((f32[32,32768]{1,0:T(8,128)}), f32[32,1024]{1,0:T(8,128)}) %reduce-scatter.2.cloned.1.call-update) | async-done | bytes 131088 | tf_op jit(solution)/shard_map/reduce_scatter | solution.py:65
  354.1 0.9 fusion.28
  355.0 0.7 slice_bitcast_fusion
  (9 shorter events, 0.0 us)
Async XLA Ops:
  7.2 15.0 %copy-start = (s32[1,24,16]{1,2,0:T(8,128)S(1)}, s32[1,24,16]{1,2,0:T(8,128)}, u32[]{:S(2)}) copy-start(s32[1,24,16]{1,2,0:T(8,128)} %param.7) | copy-start | bytes 4612
  10.7 61.5 %all-to-all-start = ((bf16[32,32,1024]{2,1,0:T(8,128)(2,1)}), bf16[32,32,1024]{2,1,0:T(8,128)(2,1)S(1)}, u32[]{:S(2)}, u32[]{:S(2)}) async-start(bf16[32,32,1024]{2,1,0:T(8,128)(2,1)} %stack.4), calls=%async_computation | async-start | bytes 4194304 | tf_op jit(solution)/shard_map/all_to_all | solution.py:32
  22.2 332.0 %reduce-scatter.2.cloned.1.call-start = ((), (), s32[]{:S(2)}) async-start(), calls=%async_computation.2 | async-start | bytes 4325376 | tf_op jit(solution)/shard_map/reduce_scatter | solution.py:65
  85.0 9.7 %copy-start.2 = (s32[1,24,128]{2,1,0:T(8,128)S(1)}, s32[1,24,128]{2,1,0:T(8,128)}, u32[]{:S(2)}) copy-start(s32[1,24,128]{2,1,0:T(8,128)} %param.8) | copy-start | bytes 36868
  132.7 221.4 %copy-start.1 = (f32[1024]{0:T(1024)S(1)}, f32[1024]{0:T(1024)}, u32[]{:S(2)}) copy-start(f32[1024]{0:T(1024)} %param.11) | copy-start | bytes 12292
  132.8 6.3 %collective-permute-start = (f32[1,32,1024]{2,1,0:T(8,128)S(1)}, f32[1,32,1024]{2,1,0:T(8,128)S(1)}, u32[]{:S(2)}, u32[]{:S(2)}) collective-permute-start(f32[1,32,1024]{2,1,0:T(8,128)S(1)} %get-tuple-element.6), channel_id=1, source_target_pairs={{0,32},{32,64},{64,96},{96,128},{128,160},{160,192},{192,224},{1,3... | collective-permute-start | bytes 393224 | tf_op jit(solution)/shard_map/ppermute | solution.py:18
  134.7 6.1 %collective-permute-start.1 = (f32[1,32,1024]{2,1,0:T(8,128)S(1)}, f32[1,32,1024]{2,1,0:T(8,128)S(1)}, u32[]{:S(2)}, u32[]{:S(2)}) collective-permute-start(f32[1,32,1024]{2,1,0:T(8,128)S(1)} %get-tuple-element.6), channel_id=1, source_target_pairs={{32,0},{64,32},{96,64},{128,96},{160,128},{192,160},{224,192},{33,... | collective-permute-start | bytes 393224 | tf_op jit(solution)/shard_map/ppermute | solution.py:20
Sparse Core Ops, SparseCore 0:
  132.9 221.1 reduce-scatter.1
